TPU v7x, 32 devices: a whole 2x2x4 slice. The times are simulated.
32 devices in a mesh: kv: 4 (over x, core), blk: 8 (over z, y).
Axes of the slice: x: 2, y: 2, z: 4, core: 2. Of those that a mesh axis runs over, the one named last changes fastest.
Arguments:
- patches: bfloat16 [24, 256, 1408], P('blk'), may hold values from -6 to 6
- merged_grid: int32 [24, 2], P('blk'), may hold values from 1 to 8, as said below
- picture_start: int32 [24], P('blk'), may hold values from 0 to 4095, as said below
- vis_gain: float32 [1408], replicated, may hold values from 0.5 to 2
- vis_qkv: bfloat16 [1408, 3, 1408], P(None, None, 'kv'), may hold values from -2 to 2
- vis_out: bfloat16 [1408, 1408], P('kv'), may hold values from -0.15625 to 0.15625
- merge_weight: bfloat16 [1408, 4096], P(None, 'kv'), may hold values from -0.15625 to 0.15625
- text_embed: bfloat16 [4096, 4096], P('blk', 'kv'), may hold values from -6 to 6
- dec_gain: float32 [4096], replicated, may hold values from 0.1 to 1.9
- w_query: bfloat16 [4096, 2048], P(None, 'kv'), may hold values from -2 to 2
- w_keyval: bfloat16 [4096, 2, 1024], P(None, None, 'kv'), may hold values from -2 to 2
- w_out: bfloat16 [2048, 4096], P('kv'), may hold values from -0.5 to 0.5
- req_lengths: int32 [8], replicated, may hold values from 1 to 2048, as said below
- final_gain: float32 [4096], P('kv'), may hold values from 0.1 to 1.9
- table: bfloat16 [8192, 4096], P('blk', 'kv'), may hold values from -0.25 to 0.25
Outputs:
- hidden: bfloat16 [4096, 4096], P('blk', 'kv')
- last_norm: bfloat16 [8, 4096], P(None, 'kv')
- max_logit: float32 [8], replicated
Inputs may be any that keep to these rules, and one draw needn't show every extreme that they name: `merged_grid`: some picture has a grid of 8 x 8 merged cells. Picture p's merged rows go to consecutive positions from picture_start[p] on, all inside the block of 512 positions with block index p // 3; pictures never share a position. `req_lengths`: the first request ends inside positions 512 to 1023; the second request holds 2048 positions, more than any other.
All inputs are finite; a program needn't handle non-finite values.
Results may differ from a plain program's by a relative error of at most 0.017.
Values may be sent and summed in bfloat16 or wider, within the bound.
No kernel may reach another device: no remote copies, remote signals or barrier semaphores. Data moves between devices by JAX's collectives and lax.ppermute only.
A program may use at most 128 MiB of HBM per device.

v0:
```python
import math
import jax
import jax.numpy as jnp
from jax import lax
from jax.sharding import PartitionSpec as P

VHD = 88
D = 4096
QHEADS = 16
KVHEADS = 8
HD = 128


def layer_norm(inputs, gain):
    centre = jnp.mean(inputs, axis=-1, keepdims=True)
    centred = inputs - centre
    spread = jnp.mean(centred * centred, axis=-1, keepdims=True)
    return centred * lax.rsqrt(spread + 1e-06) * gain


def rotate(inputs, position):
    half_width = inputs.shape[-1] // 2
    inverse = 500000.0 ** (-jnp.arange(half_width, dtype=jnp.float32) * 2.0 / inputs.shape[-1])
    angles = position.astype(jnp.float32)[:, None] * inverse[None, :]
    cosine = jnp.cos(angles)[:, None, :]
    sine = jnp.sin(angles)[:, None, :]
    first = inputs[..., :half_width]
    second = inputs[..., half_width:]
    return jnp.concatenate(
        [first * cosine - second * sine, second * cosine + first * sine], axis=-1
    )


def request_info(row_index, req_lengths):
    ends_at = jnp.cumsum(req_lengths)
    starts_at = ends_at - req_lengths
    request_id = jnp.sum((row_index[:, None] >= ends_at[None, :]).astype(jnp.int32), axis=1)
    choose = request_id[:, None] == jnp.arange(req_lengths.shape[0], dtype=jnp.int32)[None, :]
    request_begin = jnp.sum(jnp.where(choose, starts_at[None, :], 0), axis=1)
    return (request_id, request_begin)


def on_device(
    patches,
    merged_grid,
    picture_start,
    vis_gain,
    vis_qkv,
    vis_out,
    merge_weight,
    text_embed,
    dec_gain,
    w_query,
    w_keyval,
    w_out,
    req_lengths,
    final_gain,
    table,
):
    pictures, patch_max, vis_width = patches.shape
    merged_max = patch_max // 4
    vis_cols = vis_qkv.shape[2]
    vis_heads = vis_cols // VHD
    tok_rows, feat_dev = text_embed.shape
    text_rows = lax.all_gather(text_embed, "kv", axis=1, tiled=True)
    inputs = patches.astype(jnp.float32)
    normed = layer_norm(inputs, vis_gain).astype(jnp.bfloat16)
    packed = jnp.einsum(
        "pnd,dce->pnce", normed, vis_qkv, preferred_element_type=jnp.float32
    ).astype(jnp.bfloat16)
    packed = packed.reshape(pictures, patch_max, 3, vis_heads, VHD)
    scores = jnp.einsum(
        "pqhd,pkhd->phqk", packed[:, :, 0], packed[:, :, 1], preferred_element_type=jnp.float32
    ) / math.sqrt(VHD)
    cell_count = merged_grid[:, 0] * merged_grid[:, 1]
    valid_cols = jnp.arange(patch_max, dtype=jnp.int32)[None, :] < 4 * cell_count[:, None]
    scores = jnp.where(valid_cols[:, None, None, :], scores, -1e30)
    weights = jnp.exp(scores - jnp.max(scores, axis=-1, keepdims=True))
    weight_sum = jnp.sum(weights, axis=-1)
    mixed_rows = jnp.einsum(
        "phqk,pkhd->pqhd",
        weights.astype(jnp.bfloat16),
        packed[:, :, 2],
        preferred_element_type=jnp.float32,
    )
    mixed_rows = (
        (mixed_rows / jnp.transpose(weight_sum, (0, 2, 1))[..., None])
        .astype(jnp.bfloat16)
        .reshape(pictures, patch_max, vis_cols)
    )
    head_part = jnp.einsum("pnc,cd->pnd", mixed_rows, vis_out, preferred_element_type=jnp.float32)
    head_pooled = jnp.mean(head_part.reshape(pictures, merged_max, 4, vis_width), axis=2)
    head_total = lax.psum(head_pooled.astype(jnp.bfloat16), "kv").astype(jnp.float32)
    input_pooled = jnp.mean(inputs.reshape(pictures, merged_max, 4, vis_width), axis=2)
    pooled = (input_pooled + head_total).astype(jnp.bfloat16)
    merged = jnp.einsum(
        "pmd,de->pme", pooled, merge_weight, preferred_element_type=jnp.float32
    ).astype(jnp.bfloat16)
    block_base = lax.axis_index("blk") * tok_rows
    slot_index = jnp.arange(merged_max, dtype=jnp.int32)
    target = picture_start[:, None] + slot_index[None, :] - block_base
    target = jnp.where(slot_index[None, :] < cell_count[:, None], target, -1).reshape(-1)
    local_rows = jnp.arange(tok_rows, dtype=jnp.int32)
    one_hot = local_rows[:, None] == target[None, :]
    placed = jnp.dot(
        one_hot.astype(jnp.bfloat16),
        merged.reshape(pictures * merged_max, feat_dev),
        preferred_element_type=jnp.float32,
    )
    is_vision = jnp.any(one_hot, axis=1)
    seq_in = jnp.where(is_vision[:, None], placed.astype(jnp.bfloat16), text_embed)
    merged_rows = lax.all_gather(
        merged.reshape(pictures * merged_max, feat_dev), "kv", axis=1, tiled=True
    )
    placed_rows = jnp.dot(
        one_hot.astype(jnp.bfloat16), merged_rows, preferred_element_type=jnp.float32
    )
    full_rows = jnp.where(is_vision[:, None], placed_rows.astype(jnp.bfloat16), text_rows)
    full_float = full_rows.astype(jnp.float32)
    dec_normed = (
        full_float
        * lax.rsqrt(jnp.mean(full_float * full_float, axis=-1, keepdims=True) + 1e-05)
        * dec_gain
    ).astype(jnp.bfloat16)
    per_group = QHEADS // KVHEADS
    kv_heads = w_keyval.shape[2] // HD
    row_ids = block_base + local_rows
    request_id, request_begin = request_info(row_ids, req_lengths)
    position = row_ids - request_begin
    query_proj = jnp.dot(dec_normed, w_query, preferred_element_type=jnp.float32).reshape(
        tok_rows, kv_heads * per_group, HD
    )
    query_proj = (
        rotate(query_proj, position)
        .astype(jnp.bfloat16)
        .reshape(tok_rows, kv_heads * per_group * HD)
    )
    key_value = jnp.einsum("td,dce->tce", dec_normed, w_keyval, preferred_element_type=jnp.float32)
    key_rows = (
        rotate(key_value[:, 0].reshape(tok_rows, kv_heads, HD), position)
        .astype(jnp.bfloat16)
        .reshape(tok_rows, kv_heads * HD)
    )
    value_rows = key_value[:, 1].astype(jnp.bfloat16)
    query_req, query_begin = request_info(row_ids, req_lengths)
    root = math.sqrt(HD)
    reqs = req_lengths.shape[0]
    ends_at = jnp.cumsum(req_lengths)
    last_ids = ends_at - 1
    picker = (local_rows[None, :] == (last_ids - block_base)[:, None]).astype(jnp.bfloat16)
    query_last = jnp.dot(picker, query_proj, preferred_element_type=jnp.float32)
    seq_last = jnp.dot(picker, seq_in, preferred_element_type=jnp.float32)
    extras = jnp.concatenate([query_last, seq_last], axis=1).astype(jnp.bfloat16).reshape(-1)
    kv_width = key_rows.shape[1]
    ship_width = 2 * kv_width
    extra_rows = -(-extras.shape[0] // ship_width)
    extras = jnp.pad(extras, (0, extra_rows * ship_width - extras.shape[0]))
    shipped = jnp.concatenate([key_rows, value_rows], axis=1)
    shipped = jnp.concatenate([shipped, extras.reshape(extra_rows, ship_width)], axis=0)
    gathered = lax.all_gather(shipped, "blk", axis=0, tiled=False)
    blocks = gathered.shape[0]
    q_cols = query_proj.shape[1]
    extras_all = gathered[:, tok_rows:].reshape(blocks, -1)[:, : reqs * (q_cols + feat_dev)]
    extras_all = jnp.sum(extras_all.astype(jnp.float32).reshape(blocks, reqs, -1), axis=0)
    query_last = extras_all[:, :q_cols].astype(jnp.bfloat16)
    seq_last = extras_all[:, q_cols:]
    group_queries = [
        query_proj[:, g * per_group * HD : (g + 1) * per_group * HD].reshape(
            tok_rows, per_group, HD
        )
        for g in range(kv_heads)
    ]
    block_index = lax.axis_index("blk")
    first_begin = query_begin[0]

    def block_step(kb, state):
        key_first = kb * tok_rows
        needed = (kb <= block_index) & (key_first + tok_rows - 1 >= first_begin)

        def compute(state):
            piece = lax.dynamic_index_in_dim(gathered, kb, 0, keepdims=False)
            key_ids = key_first + local_rows
            key_req, unused = request_info(key_ids, req_lengths)
            allowed = (key_ids[None, :] <= row_ids[:, None]) & (
                key_req[None, :] == query_req[:, None]
            )
            allowed = allowed[:, None, :]
            new_state = []
            for g in range(kv_heads):
                run_max, run_sum, run_acc = state[g]
                keys_g = piece[:tok_rows, g * HD : (g + 1) * HD]
                values_g = piece[:tok_rows, kv_width + g * HD : kv_width + (g + 1) * HD]
                scores = (
                    jnp.einsum(
                        "tqd,kd->tqk", group_queries[g], keys_g, preferred_element_type=jnp.float32
                    )
                    / root
                )
                scores = jnp.where(allowed, scores, -1e30)
                new_max = jnp.maximum(run_max, jnp.max(scores, axis=-1))
                weights = jnp.where(allowed, jnp.exp(scores - new_max[..., None]), 0.0)
                scale = jnp.exp(run_max - new_max)
                new_sum = run_sum * scale + jnp.sum(weights, axis=-1)
                new_acc = run_acc * scale[..., None] + jnp.einsum(
                    "tqk,kd->tqd",
                    weights.astype(jnp.bfloat16),
                    values_g,
                    preferred_element_type=jnp.float32,
                )
                new_state.append((new_max, new_sum, new_acc))
            return tuple(new_state)

        return lax.cond(needed, compute, lambda s: s, state)

    init = tuple(
        (
            (
                jnp.full((tok_rows, per_group), -1e30, jnp.float32),
                jnp.zeros((tok_rows, per_group), jnp.float32),
                jnp.zeros((tok_rows, per_group, HD), jnp.float32),
            )
            for g in range(kv_heads)
        )
    )
    final = lax.fori_loop(0, blocks, block_step, init)
    context = jnp.concatenate(
        [
            (acc / total[..., None]).reshape(tok_rows, per_group * HD)
            for unused, total, acc in final
        ],
        axis=1,
    ).astype(jnp.bfloat16)
    all_ids = jnp.arange(blocks * tok_rows, dtype=jnp.int32)
    last_begin = ends_at - req_lengths
    last_allowed = (all_ids[None, :] >= last_begin[:, None]) & (
        all_ids[None, :] <= last_ids[:, None]
    )
    last_allowed = last_allowed[:, None, :]
    last_parts = []
    for g in range(kv_heads):
        keys_g = gathered[:, :tok_rows, g * HD : (g + 1) * HD].reshape(blocks * tok_rows, HD)
        values_g = gathered[:, :tok_rows, kv_width + g * HD : kv_width + (g + 1) * HD].reshape(
            blocks * tok_rows, HD
        )
        last_q = query_last[:, g * per_group * HD : (g + 1) * per_group * HD].reshape(
            reqs, per_group, HD
        )
        last_scores = (
            jnp.einsum("tqd,kd->tqk", last_q, keys_g, preferred_element_type=jnp.float32) / root
        )
        last_scores = jnp.where(last_allowed, last_scores, -1e30)
        last_max = jnp.max(last_scores, axis=-1)
        last_weights = jnp.where(last_allowed, jnp.exp(last_scores - last_max[..., None]), 0.0)
        last_sum = jnp.sum(last_weights, axis=-1)
        last_mix = jnp.einsum(
            "tqk,kd->tqd",
            last_weights.astype(jnp.bfloat16),
            values_g,
            preferred_element_type=jnp.float32,
        )
        last_parts.append((last_mix / last_sum[..., None]).reshape(reqs, per_group * HD))
    last_context = jnp.concatenate(last_parts, axis=1).astype(jnp.bfloat16)
    out_rows = jnp.concatenate([context, last_context], axis=0)
    head_sum = lax.psum_scatter(
        jnp.dot(out_rows, w_out, preferred_element_type=jnp.float32).astype(jnp.bfloat16),
        "kv",
        scatter_dimension=1,
        tiled=True,
    ).astype(jnp.float32)
    hidden = (seq_in.astype(jnp.float32) + head_sum[:tok_rows]).astype(jnp.bfloat16)
    chosen = (seq_last + head_sum[tok_rows:]).astype(jnp.bfloat16).astype(jnp.float32)
    square_part = jnp.sum(chosen * chosen, axis=-1)
    scaled = (chosen * final_gain).astype(jnp.bfloat16)
    logit_part = lax.dot_general(
        scaled, table, (((1,), (1,)), ((), ())), preferred_element_type=jnp.float32
    )
    logit_sum, square_sum = (
        lax.psum(logit_part.astype(jnp.bfloat16), "kv").astype(jnp.float32),
        lax.psum(square_part.astype(jnp.bfloat16), "kv").astype(jnp.float32),
    )
    inv_rms = lax.rsqrt(square_sum / D + 1e-05)
    last_norm = (chosen * inv_rms[:, None] * final_gain).astype(jnp.bfloat16)
    local_max = jnp.max(inv_rms[:, None] * logit_sum, axis=-1)
    max_logit = lax.pmax(local_max, "blk")
    return (hidden, last_norm, max_logit)


def solution(mesh):
    placed = (
        P("blk", None, None),
        P("blk", None),
        P("blk"),
        P(),
        P(None, None, "kv"),
        P("kv", None),
        P(None, "kv"),
        P("blk", "kv"),
        P(),
        P(None, "kv"),
        P(None, None, "kv"),
        P("kv", None),
        P(),
        P("kv"),
        P("blk", "kv"),
    )
    return jax.shard_map(
        on_device,
        mesh=mesh,
        in_specs=placed,
        out_specs=(P("blk", "kv"), P(None, "kv"), P()),
        check_vma=False,
    )
```

profile of v0, /device:TPU:0, one launch (start us, length us, event | category | flops | bytes accessed | tf_op | source)
XLA Modules:
  0.0 363.2 jit_solution(8306512292676467344)
XLA Ops:
  7.3 2.1 convert_reduce_fusion.1
  9.4 0.3 copy-done.2
  9.7 0.7 multiply_reduce_fusion
  10.5 2.9 fusion.58
  13.4 0.8 fusion.49
  14.2 0.7 fusion.50
  14.9 1.0 fusion.86
  15.9 0.6 copy.83
  16.6 0.7 dot_general.68
  17.3 1.3 convolution_reduce_fusion
  18.7 0.9 multiply_convert_fusion.1
  19.6 0.9 copy-done.3
  20.5 2.9 reshape.365
  23.4 4.8 %reduce_sum.145 = f32[3,64,1408]{2,1,0:T(8,128)S(1)} reduce(f32[3,64,4,1408]{3,2,1,0:T(4,128)} %reshape.365, f32[]{:T(128)} %constant.105.clone.1), dimensions={2}, to_apply=%region_1.0 | reduce | flops 811008 | bytes 5406724 | tf_op jit(solution)/shard_map/reduce_sum | solution.py:94
  28.2 27.3 %all-reduce.3.cloned.1.call-done = bf16[3,64,1408]{2,1,0:T(8,128)(2,1)} async-done(((bf16[3,64,1408]{2,1,0:T(8,128)(2,1)}), bf16[3,64,1408]{2,1,0:T(8,128)(2,1)}) %all-reduce.3.cloned.1.call-update) | async-done | bytes 540688 | tf_op jit(solution)/shard_map/psum | solution.py:93
  55.5 3.5 fusion.73
  59.1 0.7 all-gather.7.cloned.1.call-update
  59.8 0.2 all-gather.9.cloned.1.call-start
  60.2 0.2 reduce-window.15
  60.7 0.5 multiply_cosine_fusion
  61.3 1.6 fusion.72
  62.9 0.3 convolution_convert_fusion.4
  63.1 15.9 %all-gather.5.cloned.1.call-done = bf16[192,4096]{1,0:T(8,128)(2,1)} async-done(((bf16[192,1024]{1,0:T(8,128)(2,1)}), bf16[192,4096]{1,0:T(8,128)(2,1)}) %all-gather.5.cloned.1.call-update) | async-done | bytes 1572880 | tf_op jit(solution)/shard_map/all_gather | solution.py:112
  79.0 36.2 %all-gather.7.cloned.1.call-done = bf16[512,4096]{1,0:T(8,128)(2,1)} async-done(((bf16[512,1024]{1,0:T(8,128)(2,1)}), bf16[512,4096]{1,0:T(8,128)(2,1)}) %all-gather.7.cloned.1.call-update) | async-done | bytes 4194320 | tf_op jit(solution)/shard_map/all_gather | solution.py:65
  115.2 4.5 %fusion.30 = (f32[512]{0:T(512)S(1)}, bf16[512,4096]{1,0:T(8,128)(2,1)S(1)}) fusion(bf16[512,4096]{1,0:T(8,128)(2,1)} %all-gather.7.cloned.1.call-done, bf16[192,4096]{1,0:T(8,128)(2,1)} %all-gather.5.cloned.1.call-done, s32[192]{0:T(256)S(1)} %select_n.59, pred[512]{0:T(512)(128)(4,1)S(1)} %fusion.98), kind=kOutput, calls=%fused_computation.47 | convolution fusion | flops 815889920 | bytes 9964800 | tf_op jit(solution)/shard_map/dot_general | solution.py:115
  119.7 2.6 fusion.42
  122.4 2.6 fusion.76
  125.1 0.2 subtract_convert_fusion
  125.4 0.2 convolution_convert_fusion.5
  125.9 1.0 copy.87
  126.9 0.3 reduce-scatter.2.cloned.1.call-start
  127.2 0.5 slice.94
  127.9 0.2 copy.88
  128.0 0.2 copy.89
  128.2 74.7 %all-gather.9.cloned.1.call-done = bf16[4288,512]{1,0:T(8,128)(2,1)} async-done(((bf16[536,512]{1,0:T(8,128)(2,1)}), bf16[4288,512]{1,0:T(8,128)(2,1)}) %all-gather.9.cloned.1.call-update) | async-done | bytes 4390928 | tf_op jit(solution)/shard_map/all_gather | solution.py:160
  202.9 4.4 %fusion.120 = (bf16[8,512,128]{2,1,0:T(8,128)(2,1)}, bf16[8,512,128]{2,1,0:T(8,128)(2,1)}, bf16[8,512,128]{2,1,0:T(8,128)(2,1)}, bf16[8,512,128]{2,1,0:T(8,128)(2,1)}) fusion(bf16[8,536,512]{2,1,0:T(8,128)(2,1)} %bitcast.156), kind=kLoop, calls=%fused_computation.185 | loop fusion | bytes 8388608 | tf_op jit(solution)/shard_map/slice | solution.py:241
  207.3 1.0 convert_reduce_fusion.2
  208.2 0.8 broadcast.241
  209.1 0.8 broadcast.241.clone
  209.9 14.9 %while.28 = (s32[]{:T(128)}, f32[512,2]{0,1:T(2,128)S(1)}, f32[512,2]{0,1:T(2,128)S(1)}, f32[512,2,128]{2,0,1:T(8,128)}, f32[512,2]{0,1:T(2,128)S(1)}, /*index=5...) while((s32[]{:T(128)}, f32[512,2]{0,1:T(2,128)S(1)}, ...), condition=%wide.region_21.22_spmd.clone, body=%wide.region_12.21_spmd.clone.sunk | while | flops 551830080 | bytes 20388432 | solution.py:225
  210.6 9.5 %conditional.3 = ((f32[512,2]{0,1:T(2,128)S(1)}, f32[512,2]{0,1:T(2,128)S(1)}, f32[512,2,128]{2,0,1:T(8,128)}, f32[512,2]{0,1:T(2,128)S(1)}, f32[512,2]{0,1:T(2,128)S(1)}, /*index=5*/f32[512,2,128]{2,0,1:T(8,128)})) conditional(s32[]{:T(128)} %convert_element_type.269, (f32[512,2]{0,1:T(2,128)S(1)}, f32[512,2]{0,1:T(2,128)S(1)}, ...), branch_computations={%region_13.13_spmd, %region_14.20_spmd} | conditional | flops 551830080 | bytes 20385994 | solution.py:213
  210.6 1.1 dynamic-slice_bitcast_fusion
  211.7 0.4 fusion.21
  212.2 0.2 reduce-window.13
  212.4 0.3 compare_and_fusion
  212.7 0.8 fusion.5
  213.5 1.1 fusion.9
  214.6 2.7 convolution_add_fusion
  217.3 2.7 convolution_add_fusion.1
  224.8 1.3 copy.90
  226.1 1.2 copy.91
  227.4 1.9 fusion.123
  229.4 1.8 fusion.122
  231.2 0.2 fusion.82
  231.4 0.2 fusion.81
  232.0 6.6 %convolution_convert_fusion = bf16[520,4096]{1,0:T(8,128)(2,1)} fusion(bf16[512,4096]{1,0:T(8,128)(2,1)} %param.30, bf16[8,512]{0,1:T(8,128)(2,1)S(1)} %copy.92, bf16[512,256]{0,1:T(8,128)(2,1)S(1)} %bitcast.170, bf16[512,256]{0,1:T(8,128)(2,1)S(1)} %bitcast.171), kind=kOutput, calls=%fused_computation.50 | convolution fusion | flops 2184765440 | bytes 8986624 | tf_op jit(solution)/shard_map/dot_general | solution.py:265
  238.7 80.9 %reduce-scatter.2.cloned.1.call-done = bf16[520,1024]{1,0:T(8,128)(2,1)} async-done(((bf16[520,4096]{1,0:T(8,128)(2,1)}), bf16[520,1024]{1,0:T(8,128)(2,1)}) %reduce-scatter.2.cloned.1.call-update) | async-done | bytes 1064976 | tf_op jit(solution)/shard_map/reduce_scatter | solution.py:264
  319.5 1.6 convert_element_type.169
  321.3 1.3 fusion.57
  322.6 0.4 copy-done.8
  323.0 0.6 convolution_convert_fusion.3
  323.6 10.3 %all-reduce = (bf16[8]{0:T(256)(128)(2,1)S(1)}, bf16[8,1024]{1,0:T(8,128)(2,1)S(1)}) all-reduce(bf16[8]{0:T(256)(128)(2,1)S(1)} %get-tuple-element.768, bf16[8,1024]{1,0:T(8,128)(2,1)S(1)} %convolution_convert_fusion.3), channel_id=1, replica_groups=mesh['kv'=4,'blk'=8] {'kv'}, use_global_device_ids=true, to_apply=%region_29.30 | all-reduce | flops 8200 | bytes 32800 | tf_op jit(solution)/shard_map/psum | solution.py:279
  333.9 0.8 multiply_reduce_fusion.1
  334.7 22.0 %pmax.7 = f32[8]{0:T(128)} all-reduce(f32[8]{0:T(128)S(1)} %get-tuple-element.787), channel_id=1, replica_groups=mesh['kv'=4,'blk'=8] {'blk'}, use_global_device_ids=true, to_apply=%region_32.33 | all-reduce | flops 8 | bytes 64 | tf_op jit(solution)/shard_map/pmax | solution.py:284
  (101 shorter events, 2.2 us)
Async XLA Ops:
  7.2 3.3 copy-start
  7.2 3.2 copy-start.11
  7.2 3.3 copy-start.18
  7.2 48.3 %all-reduce.3.cloned.1.call-start = ((), (), s32[]{:S(2)}) async-start(), calls=%async_computation.1 | async-start | bytes 1081344 | tf_op jit(solution)/shard_map/psum | solution.py:93
  7.2 2.4 copy-start.2
  15.9 1.4 copy-start.16
  18.7 1.8 copy-start.3
  19.6 59.5 %all-gather.5.cloned.1.call-start = ((), (), s32[]{:S(2)}) async-start(), calls=%async_computation.2 | async-start | bytes 1966080 | tf_op jit(solution)/shard_map/all_gather | solution.py:112
  28.2 31.9 %copy-start.12 = (s32[3]{0:T(128)S(1)}, s32[3]{0:T(128)}, u32[]{:S(2)}) copy-start(s32[3]{0:T(128)} %param.21) | copy-start | bytes 40
  28.2 32.0 %copy-start.13 = (s32[8]{0:T(128)S(1)}, s32[8]{0:T(128)}, u32[]{:S(2)}) copy-start(s32[8]{0:T(128)} %param.31) | copy-start | bytes 100
  28.2 33.1 %copy-start.9 = (bf16[512,1024]{1,0:T(8,128)(2,1)S(1)}, bf16[512,1024]{1,0:T(8,128)(2,1)}, u32[]{:S(2)}) copy-start(bf16[512,1024]{1,0:T(8,128)(2,1)} %param.26) | copy-start | bytes 3145732
  59.1 56.1 %all-gather.7.cloned.1.call-start = ((), (), s32[]{:S(2)}) async-start(), calls=%async_computation.3 | async-start | bytes 5242880 | tf_op jit(solution)/shard_map/all_gather | solution.py:65
  59.8 143.1 %all-gather.9.cloned.1.call-start = ((), (), s32[]{:S(2)}) async-start(), calls=%async_computation.5 | async-start | bytes 4939776 | tf_op jit(solution)/shard_map/all_gather | solution.py:160
  62.8 56.8 %copy-start.4 = (bf16[512,1024]{1,0:T(8,128)(2,1)}, bf16[512,1024]{1,0:T(8,128)(2,1)S(1)}, u32[]{:S(2)}) copy-start(bf16[512,1024]{1,0:T(8,128)(2,1)S(1)} %fusion.72) | copy-start | bytes 3145732
  63.1 56.5 %copy-start.17 = (f32[4096]{0:T(1024)S(1)}, f32[4096]{0:T(1024)}, u32[]{:S(2)}) copy-start(f32[4096]{0:T(1024)} %param.27) | copy-start | bytes 49156
  115.2 4.5 %copy-start.14 = (bf16[4096,2,256]{2,1,0:T(2,128)(2,1)S(1)}, bf16[4096,2,256]{2,1,0:T(2,128)(2,1)}, u32[]{:S(2)}) copy-start(bf16[4096,2,256]{2,1,0:T(2,128)(2,1)} %param.29) | copy-start | bytes 12582916
  119.7 2.7 copy-start.15
  126.9 192.6 %reduce-scatter.2.cloned.1.call-start = ((), (), s32[]{:S(2)}) async-start(), calls=%async_computation.4 | async-start | bytes 5324800 | tf_op jit(solution)/shard_map/reduce_scatter | solution.py:264
  224.8 6.4 %copy-start.7 = (bf16[8,512,128]{2,1,0:T(8,128)(2,1)S(1)}, bf16[8,512,128]{2,1,0:T(8,128)(2,1)}, u32[]{:S(2)}) copy-start(bf16[8,512,128]{2,1,0:T(8,128)(2,1)} %get-tuple-element.776) | copy-start | bytes 3145732
  227.4 4.1 %copy-start.6 = (bf16[8,512,128]{2,1,0:T(8,128)(2,1)S(1)}, bf16[8,512,128]{2,1,0:T(8,128)(2,1)}, u32[]{:S(2)}) copy-start(bf16[8,512,128]{2,1,0:T(8,128)(2,1)} %get-tuple-element.774) | copy-start | bytes 3145732
  319.5 1.7 copy-start.5
  321.1 1.9 copy-start.8
  321.1 1.8 copy-start.10
  321.3 35.4 %copy-start.1 = (bf16[1408,3,352]{0,2,1:T(8,128)(2,1)S(1)}, bf16[1408,3,352]{0,2,1:T(8,128)(2,1)}, u32[]{:S(2)}) copy-start(bf16[1408,3,352]{0,2,1:T(8,128)(2,1)} %param.23) | copy-start | bytes 8921092
Sparse Core Ops, SparseCore 0:
  19.7 35.7 all-reduce.2
  59.2 19.7 all-gather.4
  80.7 34.4 all-gather.6
  127.0 75.8 all-gather.8
  238.8 80.7 reduce-scatter.1
where the time goes:
time: 364 us; the launch traced here: 363 us
  waiting for transfers between devices  236 us (65%)
  matrix products  39.4 us (11%)
  blocking collectives  32.2 us (9%)
  local copies, waits for them, and re-layouts  18 us (5%)
  other arithmetic  17.5 us (5%)
  between operations  14.3 us (4%)
  loops' own time  5.47 us (2%)
    reduce_scatter x1, waiting for transfers between devices, on_device(): lax.psum_scatter(jnp.dot(out_rows, w_out, preferred_element_type=jnp.floa...  80.9 us
    all_gather x1, waiting for transfers between devices, on_device(): gathered = lax.all_gather(shipped, 'blk', axis=0, tiled=False)  74.7 us
    all_gather x1, waiting for transfers between devices, on_device(): text_rows = lax.all_gather(text_embed, 'kv', axis=1, tiled=True)  36.2 us
    psum x1, waiting for transfers between devices, on_device(): lax.psum(head_pooled.astype(jnp.bfloat16), 'kv').astype(jnp.float32)  27.3 us
    pmax x1, blocking collectives, on_device(): max_logit = lax.pmax(local_max, 'blk')  22 us
    all_gather x1, waiting for transfers between devices, on_device(): lax.all_gather(merged.reshape(pictures * merged_max, feat_dev), 'kv', axi...  15.9 us
    psum x1, blocking collectives, on_device(): lax.psum(square_part.astype(jnp.bfloat16), 'kv').astype(jnp.float32)  10.3 us
  transfers between devices with their start and end apart: 5, of which 5 were waited for; matrix products, arithmetic and copies ran while one was open for 3% of the time, Pallas kernels for 0%

commit v1 on v0

--- a/solution.py
+++ b/solution.py
@@ -57,12 +57,25 @@
     final_gain,
     table,
 ):
+
+    def supply_views_by_axis(xin, axis_name, dim_k):
+        world_n = lax.axis_size(axis_name)
+        outcome_arr = sorted(((ii, (ii + 1) % world_n) for ii in range(world_n)))
+        block_now = xin
+        buffers = [block_now]
+        for j in range(1, world_n):
+            block_now = lax.ppermute(block_now, axis_name, outcome_arr)
+            buffers.insert(0, block_now)
+        last = jnp.concatenate(buffers, axis=dim_k)
+        base_arr = lax.axis_index(axis_name)
+        return jnp.roll(last, (base_arr + 1) * xin.shape[dim_k], dim_k)
+
     pictures, patch_max, vis_width = patches.shape
     merged_max = patch_max // 4
     vis_cols = vis_qkv.shape[2]
     vis_heads = vis_cols // VHD
     tok_rows, feat_dev = text_embed.shape
-    text_rows = lax.all_gather(text_embed, "kv", axis=1, tiled=True)
+    text_rows = supply_views_by_axis(text_embed, "kv", 1)
     inputs = patches.astype(jnp.float32)
     normed = layer_norm(inputs, vis_gain).astype(jnp.bfloat16)
     packed = jnp.einsum(

time: 364 us -> 328 us (0.901)
  waiting for transfers between devices: 236 us -> 189 us
  local copies, waits for them, and re-layouts: 18 us -> 26.1 us
    all_gather x1 -> x0, waiting for transfers between devices: 36.2 us -> none  [on_device(): text_rows = lax.all_gather(text_embed, 'kv', axis=1, tiled=True)]
    ppermute x0 -> x3, waiting for transfers between devices: none -> 20.6 us  [supply_views_by_axis(): block_now = lax.ppermute(block_now, axis_name, outcome_arr)]
    all_gather x1, waiting for transfers between devices: 15.9 us -> 0.01 us  [on_device(): lax.all_gather(merged.reshape(pictures * merged_max, feat_dev), 'kv', axi...]
    reduce_scatter x1, waiting for transfers between devices: 80.9 us -> 66.9 us  [on_device(): lax.psum_scatter(jnp.dot(out_rows, w_out, preferred_element_type=jnp.floa...]
    unnamed x40 -> x39, local copies, waits for them, and re-layouts: 1.94 us -> 12.8 us
  transfers between devices with their start and end apart: 5 -> 7, of which waited for: 5 -> 5; matrix products, arithmetic and copies ran while one was open for 3% -> 13% of each run, Pallas kernels for 0% -> 0%
where the time goes in v1:
time: 328 us; the launch traced here: 327 us
  waiting for transfers between devices  189 us (58%)
  matrix products  37.2 us (11%)
  blocking collectives  32.2 us (10%)
  local copies, waits for them, and re-layouts  26.1 us (8%)
  other arithmetic  19.8 us (6%)
  between operations  14.3 us (4%)
  loops' own time  4.93 us (2%)
  starting transfers between devices  3.29 us (1%)
    all_gather x1, waiting for transfers between devices, on_device(): gathered = lax.all_gather(shipped, 'blk', axis=0, tiled=False)  74.9 us
    reduce_scatter x1, waiting for transfers between devices, on_device(): lax.psum_scatter(jnp.dot(out_rows, w_out, preferred_element_type=jnp.floa...  66.9 us
    psum x1, waiting for transfers between devices, on_device(): lax.psum(head_pooled.astype(jnp.bfloat16), 'kv').astype(jnp.float32)  26.7 us
    pmax x1, blocking collectives, on_device(): max_logit = lax.pmax(local_max, 'blk')  22 us
    ppermute x3, waiting for transfers between devices, supply_views_by_axis(): block_now = lax.ppermute(block_now, axis_name, outcome_arr)  20.6 us
    unnamed x39, local copies, waits for them, and re-layouts  12.8 us
    psum x1, blocking collectives, on_device(): lax.psum(square_part.astype(jnp.bfloat16), 'kv').astype(jnp.float32)  10.3 us
    dot_general x1, matrix products, on_device(): jnp.dot(out_rows, w_out, preferred_element_type=jnp.float32)  6.57 us
  transfers between devices with their start and end apart: 7, of which 5 were waited for; matrix products, arithmetic and copies ran while one was open for 13% of the time, Pallas kernels for 0%

profile of v1, /device:TPU:0, one launch (start us, length us, event | category | flops | bytes accessed | tf_op | source)
XLA Modules:
  0.0 327.0 jit_solution(11259035031260827775)
XLA Ops:
  7.2 0.5 collective-permute-start
  7.8 1.0 fusion.117
  8.8 2.0 convert_reduce_fusion.1
  10.8 0.7 multiply_reduce_fusion
  11.5 2.9 fusion.57
  14.4 0.8 fusion.48
  15.2 0.7 fusion.49
  16.0 1.0 fusion.85
  17.0 0.6 copy.83
  17.6 0.7 dot_general.68
  18.4 2.7 convolution_reduce_fusion
  21.1 0.9 multiply_convert_fusion.1
  22.3 0.2 collective-permute-done
  22.5 2.2 collective-permute-start.1
  24.7 2.9 reshape.365
  27.6 4.8 %reduce_sum.145 = f32[3,64,1408]{2,1,0:T(8,128)S(1)} reduce(f32[3,64,4,1408]{3,2,1,0:T(4,128)} %reshape.365, f32[]{:T(128)} %constant.128.clone.1), dimensions={2}, to_apply=%region_1.2 | reduce | flops 811008 | bytes 5406724 | tf_op jit(solution)/shard_map/reduce_sum | solution.py:107
  32.5 26.7 %all-reduce.3.cloned.1.call-done = bf16[3,64,1408]{2,1,0:T(8,128)(2,1)} async-done(((bf16[3,64,1408]{2,1,0:T(8,128)(2,1)}), bf16[3,64,1408]{2,1,0:T(8,128)(2,1)}) %all-reduce.3.cloned.1.call-update) | async-done | bytes 540688 | tf_op jit(solution)/shard_map/psum | solution.py:106
  59.3 3.5 %fusion.72 = bf16[3,64,1024]{2,1,0:T(8,128)(2,1)} fusion(bf16[1408,1024]{1,0:T(8,128)(2,1)} %param.25, bf16[3,64,1408]{2,1,0:T(8,128)(2,1)} %all-reduce.3.cloned.1.call-done, f32[3,64,1408]{2,1,0:T(8,128)S(1)} %reduce_sum.145), kind=kOutput, calls=%fused_computation.94 | convolution fusion | flops 554926080 | bytes 4898816 | tf_op jit(solution)/shard_map/pmd,de->pme/dot_general | solution.py:109
  63.2 0.2 collective-permute-start.2
  63.5 0.5 multiply_cosine_fusion
  64.0 1.6 fusion.71
  65.6 0.3 convolution_convert_fusion.4
  65.9 20.4 %collective-permute-done.2 = bf16[512,1024]{1,0:T(8,128)(2,1)S(1)} collective-permute-done((bf16[512,1024]{1,0:T(8,128)(2,1)}, bf16[512,1024]{1,0:T(8,128)(2,1)S(1)}, u32[]{:S(2)}, u32[]{:S(2)}) %collective-permute-start.2) | collective-permute-done | bytes 1048608 | tf_op jit(solution)/shard_map/ppermute | solution.py:67
  86.3 1.1 constant_dynamic-update-slice_fusion.7
  87.4 2.4 constant_dynamic-update-slice_fusion.6
  89.7 2.3 constant_dynamic-update-slice_fusion.5
  92.0 1.0 constant_dynamic-update-slice_fusion.4
  93.1 1.1 constant_dynamic-update-slice_fusion.3
  94.1 2.3 constant_dynamic-update-slice_fusion.2
  96.4 2.3 constant_dynamic-update-slice_fusion.1
  98.7 1.1 constant_dynamic-update-slice_fusion
  99.8 4.5 %fusion.30 = (f32[512]{0:T(512)S(1)}, bf16[512,4096]{1,0:T(8,128)(2,1)S(1)}) fusion(bf16[512,8192]{1,0:T(8,128)(2,1)} %constant_dynamic-update-slice_fusion, s32[]{:T(128)S(6)} %select_n.77, bf16[192,4096]{1,0:T(8,128)(2,1)} %all-gather.4.cloned.1.call-done, s32[192]{0:T(256)S(1)} %select_n.72, pred[512]{0:T(512)(128)(4,1)S(1)} %fusion.97), kind=kOutput, calls=%fused_computation.47 | convolution fusion | flops 815889920 | bytes 9964804 | tf_op jit(solution)/shard_map/dot_general | solution.py:128
  104.3 2.6 fusion.41
  107.0 2.6 fusion.75
  109.8 0.2 convolution_convert_fusion.5
  110.3 0.4 slice-done
  110.8 1.0 copy.87
  111.9 0.3 reduce-scatter.2.cloned.1.call-start
  112.2 0.5 slice.94
  113.1 74.9 %all-gather.6.cloned.1.call-done = bf16[4288,512]{1,0:T(8,128)(2,1)} async-done(((bf16[536,512]{1,0:T(8,128)(2,1)}), bf16[4288,512]{1,0:T(8,128)(2,1)}) %all-gather.6.cloned.1.call-update) | async-done | bytes 4390928 | tf_op jit(solution)/shard_map/all_gather | solution.py:173
  188.0 3.9 %fusion.119 = (bf16[8,512,128]{2,1,0:T(8,128)(2,1)}, bf16[8,512,128]{2,1,0:T(8,128)(2,1)S(1)}, bf16[8,512,128]{2,1,0:T(8,128)(2,1)}, bf16[8,512,128]{2,1,0:T(8,128)(2,1)S(1)}) fusion(bf16[8,536,512]{2,1,0:T(8,128)(2,1)} %bitcast.156), kind=kLoop, calls=%fused_computation.193 | loop fusion | bytes 8388608 | tf_op jit(solution)/shard_map/slice | solution.py:254
  192.0 1.0 convert_reduce_fusion.2
  193.0 1.8 fusion.121
  194.8 1.8 fusion.122
  196.6 0.2 fusion.80
  196.9 0.3 fusion.81
  197.4 10.8 %while.28 = (s32[]{:T(128)}, f32[512,2]{0,1:T(2,128)S(1)}, f32[512,2]{0,1:T(2,128)S(1)}, f32[512,2,128]{2,0,1:T(8,128)S(1)}, f32[512,2]{0,1:T(2,128)S(1)}, /*ind...) while((s32[]{:T(128)}, f32[512,2]{0,1:T(2,128)S(1)}, ...), condition=%wide.region_21.22_spmd.clone, body=%wide.region_12.21_spmd.clone.sunk | while | flops 551830080 | bytes 20388440 | solution.py:238
  198.0 5.9 %conditional.3 = ((f32[512,2]{0,1:T(2,128)S(1)}, f32[512,2]{0,1:T(2,128)S(1)}, f32[512,2,128]{2,0,1:T(8,128)S(1)}, f32[512,2]{0,1:T(2,128)S(1)}, f32[512,2]{0,1:T(2,128)S(1)}, /*index=5*/f32[512,2,128]{2,0,1:T(8,128)S(1)})) conditional(s32[]{:T(128)} %convert_element_type.269, (f32[512,2]{0,1:T(2,128)S(1)}, f32[512,2]{0,1:T(2,128)S(1)}, ...), branch_computations={%region_13.13_spmd, %region_14.20_spmd} | conditional | flops 551830080 | bytes 20385994 | solution.py:226
  198.3 0.3 compare_and_fusion
  198.6 1.1 dynamic-slice_bitcast_fusion
  199.7 0.4 fusion.21
  200.2 0.8 fusion.5
  201.0 1.0 fusion.9
  202.1 0.9 convolution_add_fusion.1
  203.0 0.9 convolution_add_fusion
  208.2 0.2 copy.91
  208.8 6.6 %convolution_convert_fusion = bf16[520,4096]{1,0:T(8,128)(2,1)} fusion(bf16[512,4096]{1,0:T(8,128)(2,1)} %param.30, bf16[8,512]{0,1:T(8,128)(2,1)S(1)} %copy.92, bf16[512,256]{0,1:T(8,128)(2,1)S(1)} %bitcast.170, bf16[512,256]{0,1:T(8,128)(2,1)S(1)} %bitcast.171), kind=kOutput, calls=%fused_computation.50 | convolution fusion | flops 2184765440 | bytes 8986624 | tf_op jit(solution)/shard_map/dot_general | solution.py:278
  215.4 66.9 %reduce-scatter.2.cloned.1.call-done = bf16[520,1024]{1,0:T(8,128)(2,1)} async-done(((bf16[520,4096]{1,0:T(8,128)(2,1)}), bf16[520,1024]{1,0:T(8,128)(2,1)}) %reduce-scatter.2.cloned.1.call-update) | async-done | bytes 1064976 | tf_op jit(solution)/shard_map/reduce_scatter | solution.py:277
  282.3 1.6 convert_element_type.169
  283.9 2.7 fusion.56
  286.8 0.6 convolution_convert_fusion.3
  287.5 10.3 %all-reduce = (bf16[8]{0:T(256)(128)(2,1)S(1)}, bf16[8,1024]{1,0:T(8,128)(2,1)S(1)}) all-reduce(bf16[8]{0:T(256)(128)(2,1)S(1)} %get-tuple-element.768, bf16[8,1024]{1,0:T(8,128)(2,1)S(1)} %convolution_convert_fusion.3), channel_id=1, replica_groups=mesh['kv'=4,'blk'=8] {'kv'}, use_global_device_ids=true, to_apply=%region_29.30 | all-reduce | flops 8200 | bytes 32800 | tf_op jit(solution)/shard_map/psum | solution.py:292
  297.7 0.8 multiply_reduce_fusion.1
  298.5 22.0 %pmax.7 = f32[8]{0:T(128)} all-reduce(f32[8]{0:T(128)S(1)} %get-tuple-element.787), channel_id=1, replica_groups=mesh['kv'=4,'blk'=8] {'blk'}, use_global_device_ids=true, to_apply=%region_32.33 | all-reduce | flops 8 | bytes 64 | tf_op jit(solution)/shard_map/pmax | solution.py:297
  (105 shorter events, 3.3 us)
Async XLA Ops:
  7.2 4.4 %copy-start = (bf16[1408,3,352]{0,2,1:T(8,128)(2,1)S(1)}, bf16[1408,3,352]{0,2,1:T(8,128)(2,1)}, u32[]{:S(2)}) copy-start(bf16[1408,3,352]{0,2,1:T(8,128)(2,1)} %param.23) | copy-start | bytes 8921092
  7.2 4.3 %copy-start.14 = (f32[1408]{0:T(1024)S(1)}, f32[1408]{0:T(1024)}, u32[]{:S(2)}) copy-start(f32[1408]{0:T(1024)} %param.22) | copy-start | bytes 16900
  7.2 52.1 %all-reduce.3.cloned.1.call-start = ((), (), s32[]{:S(2)}) async-start(), calls=%async_computation.1 | async-start | bytes 1081344 | tf_op jit(solution)/shard_map/psum | solution.py:106
  7.2 3.6 %copy-start.2 = (bf16[3,256,1408]{2,1,0:T(8,128)(2,1)S(1)}, bf16[3,256,1408]{2,1,0:T(8,128)(2,1)}, u32[]{:S(2)}) copy-start(bf16[3,256,1408]{2,1,0:T(8,128)(2,1)} %param.19) | copy-start | bytes 6488068
  7.2 15.2 %collective-permute-start = (bf16[512,1024]{1,0:T(8,128)(2,1)}, bf16[512,1024]{1,0:T(8,128)(2,1)}, u32[]{:S(2)}, u32[]{:S(2)}) collective-permute-start(bf16[512,1024]{1,0:T(8,128)(2,1)} %param.26), channel_id=1, source_target_pairs={{0,8},{8,16},{16,24},{24,0},{1,9},{9,17},{17,25},{25,1},{2,10},{10... | collective-permute-start | bytes 3145736 | tf_op jit(solution)/shard_map/ppermute | solution.py:67
  18.4 3.7 %copy-start.10 = (s32[8]{0:T(128)S(1)}, s32[8]{0:T(128)}, u32[]{:S(2)}) copy-start(s32[8]{0:T(128)} %param.31) | copy-start | bytes 100
  18.4 6.4 %copy-start.3 = (bf16[3,256,1408]{2,1,0:T(8,128)(2,1)S(1)}, bf16[3,256,1408]{2,1,0:T(8,128)(2,1)}, u32[]{:S(2)}) copy-start(bf16[3,256,1408]{2,1,0:T(8,128)(2,1)} %param.19) | copy-start | bytes 6488068
  22.0 77.7 %all-gather.4.cloned.1.call-start = ((), (), s32[]{:S(2)}) async-start(), calls=%async_computation.2 | async-start | bytes 1966080 | tf_op jit(solution)/shard_map/all_gather | solution.py:125
  22.5 40.7 %collective-permute-start.1 = (bf16[512,1024]{1,0:T(8,128)(2,1)}, bf16[512,1024]{1,0:T(8,128)(2,1)}, u32[]{:S(2)}, u32[]{:S(2)}) collective-permute-start(bf16[512,1024]{1,0:T(8,128)(2,1)} %collective-permute-done), channel_id=1, source_target_pairs={{0,8},{8,16},{16,24},{24,0},{1,9},{9,17},{17,25},{25,1},{2,10},{10... | collective-permute-start | bytes 3145736 | tf_op jit(solution)/shard_map/ppermute | solution.py:67
  27.6 4.8 %copy-start.9 = (s32[3]{0:T(128)S(1)}, s32[3]{0:T(128)}, u32[]{:S(2)}) copy-start(s32[3]{0:T(128)} %param.21) | copy-start | bytes 40
  32.4 31.6 %copy-start.4 = (bf16[512,1024]{1,0:T(8,128)(2,1)S(1)}, bf16[512,1024]{1,0:T(8,128)(2,1)}, u32[]{:S(2)}) copy-start(bf16[512,1024]{1,0:T(8,128)(2,1)} %param.26) | copy-start | bytes 3145732
  62.8 125.2 %all-gather.6.cloned.1.call-start = ((), (), s32[]{:S(2)}) async-start(), calls=%async_computation.4 | async-start | bytes 4939776 | tf_op jit(solution)/shard_map/all_gather | solution.py:173
  63.2 23.1 %collective-permute-start.2 = (bf16[512,1024]{1,0:T(8,128)(2,1)}, bf16[512,1024]{1,0:T(8,128)(2,1)S(1)}, u32[]{:S(2)}, u32[]{:S(2)}) collective-permute-start(bf16[512,1024]{1,0:T(8,128)(2,1)} %collective-permute-done.1), channel_id=1, source_target_pairs={{0,8},{8,16},{16,24},{24,0},{1,9},{9,17},{17,25},{25,1},{2,10},{10... | collective-permute-start | bytes 3145736 | tf_op jit(solution)/shard_map/ppermute | solution.py:67
  65.6 26.4 %copy-start.5 = (bf16[512,1024]{1,0:T(8,128)(2,1)}, bf16[512,1024]{1,0:T(8,128)(2,1)S(1)}, u32[]{:S(2)}) copy-start(bf16[512,1024]{1,0:T(8,128)(2,1)S(1)} %fusion.71) | copy-start | bytes 3145732
  99.8 4.5 %copy-start.13 = (f32[4096]{0:T(1024)S(1)}, f32[4096]{0:T(1024)}, u32[]{:S(2)}) copy-start(f32[4096]{0:T(1024)} %param.27) | copy-start | bytes 49156
  99.8 4.5 %copy-start.11 = (bf16[4096,2,256]{2,1,0:T(2,128)(2,1)S(1)}, bf16[4096,2,256]{2,1,0:T(2,128)(2,1)}, u32[]{:S(2)}) copy-start(bf16[4096,2,256]{2,1,0:T(2,128)(2,1)} %param.29) | copy-start | bytes 12582916
  104.3 2.7 copy-start.12
  106.9 2.7 copy-start.7
  109.6 1.0 slice-start
  111.9 170.4 %reduce-scatter.2.cloned.1.call-start = ((), (), s32[]{:S(2)}) async-start(), calls=%async_computation.3 | async-start | bytes 5324800 | tf_op jit(solution)/shard_map/reduce_scatter | solution.py:277
  215.4 71.4 %copy-start.8 = (f32[1024]{0:T(1024)S(1)}, f32[1024]{0:T(1024)}, u32[]{:S(2)}) copy-start(f32[1024]{0:T(1024)} %param.32) | copy-start | bytes 12292
  282.3 4.5 %copy-start.6 = (bf16[1024,1024]{1,0:T(8,128)(2,1)S(1)}, bf16[1024,1024]{1,0:T(8,128)(2,1)}, u32[]{:S(2)}) copy-start(bf16[1024,1024]{1,0:T(8,128)(2,1)} %param.33) | copy-start | bytes 6291460
  282.3 38.2 %copy-start.1 = (bf16[1408,3,352]{0,2,1:T(8,128)(2,1)S(1)}, bf16[1408,3,352]{0,2,1:T(8,128)(2,1)}, u32[]{:S(2)}) copy-start(bf16[1408,3,352]{0,2,1:T(8,128)(2,1)} %param.23) | copy-start | bytes 8921092
Sparse Core Ops, SparseCore 0:
  22.1 37.0 all-reduce.2
  62.9 24.0 all-gather.3
  112.0 75.9 all-gather.5
  215.5 66.7 reduce-scatter.1
